TPU v7x, 32 devices: a whole 2x2x4 slice. The times are simulated.
32 devices in a mesh: rep: 2 (over x), member: 4 (over y, core), tp: 4 (over z).
Axes of the slice: x: 2, y: 2, z: 4, core: 2. Of those that a mesh axis runs over, the one named last changes fastest.
Arguments:
- states: bfloat16 [4096, 1024], P(('rep', 'member', 'tp')), parts along dimension 0, may hold values from -6 to 6
- member_of: int32 [4096, 1], P(('rep', 'member', 'tp')), parts along dimension 0, may hold values from 0 to 1; in each aligned block of 128 rows (0 to 127, 128 to 255, ...) at most 128 rows name the same one
- place: int32 [4096], P(('rep', 'member', 'tp')), parts along dimension 0, may hold values from 0 to 2047, as said below
- norm_gain: float32 [2, 1024], replicated, may hold values from 0.5 to 2
- w_up: bfloat16 [4, 1024, 2048], P('member', None, 'tp'), may hold values from -0.1875 to 0.1875
- w_down: bfloat16 [4, 2048, 1024], P('member', 'tp'), may hold values from -0.09375 to 0.09375
- policy_gain: float32 [1024], replicated, may hold values from 0.5 to 2
- w_policy: bfloat16 [1024, 128], replicated, may hold values from -0.1875 to 0.1875
Outputs:
- imagined: bfloat16 [4096, 1024], P(('rep', 'member', 'tp')), parts along dimension 0
- action: bfloat16 [4096, 128], P(('rep', 'member', 'tp')), parts along dimension 0
There are 2 independent parts, one for each index of `rep`. A program takes and returns all parts, laid end to end along the dimension named above; an argument that names none is the same for every part. Nothing has to cross between parts.
Inputs may be any that keep to these rules, and one draw needn't show every extreme that they name: `member_of`: at most 128 of the rows of one device name any one member, and that count is reached on some device. `place`: A permutation of the 2048 learner positions; learner device k holds positions k * 128 to (k + 1) * 128 - 1, and the rows of each device go exactly 8 to every learner device.
All inputs are finite; a program needn't handle non-finite values.
Results may differ from a plain program's by a relative error of at most 0.0069.
Values may be sent and summed in bfloat16 or wider, within the bound.
No kernel may reach another device: no remote copies, remote signals or barrier semaphores. Data moves between devices by JAX's collectives and lax.ppermute only.
A program may use at most 128 MiB of HBM per device.

v0:
```python
import jax
import jax.numpy as jnp
from jax import lax
from jax.sharding import PartitionSpec as P

PARTIAL_DTYPE = jnp.bfloat16


def from_partner(value, axis, distance):
    return lax.ppermute(value, axis, [(i, i ^ 1 << distance) for i in range(lax.axis_size(axis))])


def from_chip_behind(value, axis, chips_back):
    size = lax.axis_size(axis)
    return lax.ppermute(value, axis, [(i, (i + 2 * chips_back) % size) for i in range(size)])


def swap_parts(value):
    n_rep = lax.axis_size("rep")
    return [value] + [
        lax.ppermute(value, "rep", [(i, (i + step) % n_rep) for i in range(n_rep)])
        for step in range(1, n_rep)
    ]


def fetch_shared(up, down, chips_back):
    n_rep = lax.axis_size("rep")
    share = up.shape[1] // n_rep
    rep_here = lax.axis_index("rep")
    got_up = from_chip_behind(
        lax.dynamic_slice_in_dim(up, rep_here * share, share, axis=1), "member", chips_back
    )
    got_up, down = lax.optimization_barrier((got_up, down))
    got_down = from_chip_behind(
        lax.dynamic_slice_in_dim(down, rep_here * share, share, axis=0), "member", chips_back
    )
    up_parts = swap_parts(got_up)
    down_parts = swap_parts(got_down)
    partner_up = [from_partner(part, "member", 0) for part in up_parts]
    partner_down = [from_partner(part, "member", 0) for part in down_parts]
    return (up_parts + partner_up, down_parts + partner_down)


def rms_scale(values, gain):
    mean_square = jnp.mean(values * values, axis=-1, keepdims=True)
    return values * lax.rsqrt(mean_square + 1e-06) * gain


def running_rank(member_hits):
    return jnp.sum((jnp.cumsum(member_hits, axis=0) - member_hits) * member_hits, axis=1)


def local(states, member_of, place, norm_gain, w_up, w_down, policy_gain, w_policy):
    n_member = lax.axis_size("member")
    n_tp = lax.axis_size("tp")
    n_dev = n_member * n_tp
    member_total = n_member // 2
    rows_here = states.shape[0]
    feature_width = states.shape[1]
    own_member = lax.axis_index("member") // 2
    own_block = (own_member, w_up[0], w_down[0])
    fetched = [
        ((own_member - back + member_total) % member_total, *fetch_shared(w_up[0], w_down[0], back))
        for back in range(1, member_total)
    ]
    per_learner = rows_here // n_dev
    learner = place // rows_here
    learner_hits = (learner[:, None] == jnp.arange(n_dev, dtype=jnp.int32)[None, :]).astype(
        jnp.int32
    )
    lane_index = learner * per_learner + running_rank(learner_hits)
    placer = jnp.arange(rows_here, dtype=jnp.int32)[:, None] == lane_index[None, :]
    states = jnp.dot(
        placer.astype(jnp.bfloat16), states, preferred_element_type=jnp.float32
    ).astype(jnp.bfloat16)
    member = jnp.sum(placer.astype(jnp.int32) * member_of[:, 0][None, :], axis=1)
    packed_spot = jnp.sum(placer.astype(jnp.int32) * (place % rows_here)[None, :], axis=1)
    gain_rows = jnp.take(norm_gain, member, axis=0)
    normed = rms_scale(states.astype(jnp.float32), gain_rows).astype(jnp.bfloat16)
    member_lanes = jnp.where(
        jnp.arange(128, dtype=jnp.int32)[None, :] == 0, member[:, None], 0
    ).astype(jnp.bfloat16)
    gathered = lax.all_gather(
        jnp.concatenate([normed, member_lanes], axis=1), "tp", axis=0, tiled=True
    )
    gathered_rows = gathered[:, :feature_width]
    gathered_member = gathered[:, feature_width].astype(jnp.int32)

    def apply_block(block_member, up_here, down_here):
        keep = (gathered_member == block_member).astype(jnp.bfloat16)[:, None]
        hidden = (
            jax.nn.gelu(jnp.dot(gathered_rows, up_here, preferred_element_type=jnp.float32)).astype(
                jnp.bfloat16
            )
            * keep
        )
        return jnp.dot(hidden, down_here, preferred_element_type=jnp.float32)

    def apply_pair(block_member, up_here, down_here):
        both_up = jnp.concatenate([up_here, from_partner(up_here, "member", 0)], axis=1)
        both_down = jnp.concatenate([down_here, from_partner(down_here, "member", 0)], axis=0)
        return apply_block(block_member, both_up, both_down)

    terms = [apply_pair(*own_block)]
    for block_member, up_here, down_here in fetched:
        terms, up_here, down_here = lax.optimization_barrier((terms, up_here, down_here))
        terms = terms + [
            apply_block(
                block_member, jnp.concatenate(up_here, axis=1), jnp.concatenate(down_here, axis=0)
            )
        ]
    tp_here = lax.axis_index("tp")
    by_target = [term.reshape(n_tp, rows_here, feature_width) for term in terms]

    def slice_for(target):
        pieces = [lax.dynamic_index_in_dim(term, target, 0, keepdims=False) for term in by_target]
        total = pieces[0]
        for piece in pieces[1:]:
            total = total + piece
        return total

    change = slice_for(tp_here)
    for shift in range(1, n_tp):
        change = change + lax.ppermute(
            slice_for((tp_here + shift) % n_tp).astype(PARTIAL_DTYPE),
            "tp",
            [(i, (i + shift) % n_tp) for i in range(n_tp)],
        ).astype(jnp.float32)
    packed = (states.astype(jnp.float32) + change).astype(jnp.bfloat16)
    spot_lanes = jnp.where(
        jnp.arange(128, dtype=jnp.int32)[None, :] == 0, packed_spot[:, None], 0
    ).astype(jnp.bfloat16)
    arrivals = lax.all_to_all(
        jnp.concatenate([packed, spot_lanes], axis=1).reshape(
            n_dev, per_learner, feature_width + 128
        ),
        ("member", "tp"),
        split_axis=0,
        concat_axis=0,
        tiled=True,
    )
    arrivals = arrivals.reshape(n_dev * per_learner, feature_width + 128)
    arrival_spots = arrivals[:, feature_width].astype(jnp.int32)
    settle = (jnp.arange(rows_here, dtype=jnp.int32)[:, None] == arrival_spots[None, :]).astype(
        jnp.bfloat16
    )
    imagined = jnp.dot(
        settle, arrivals[:, :feature_width], preferred_element_type=jnp.float32
    ).astype(jnp.bfloat16)
    policy_normed = rms_scale(imagined.astype(jnp.float32), policy_gain).astype(jnp.bfloat16)
    action = jnp.tanh(jnp.dot(policy_normed, w_policy, preferred_element_type=jnp.float32)).astype(
        jnp.bfloat16
    )
    return (imagined, action)


def solution(mesh):
    in_specs = (
        P(("rep", "member", "tp"), None),
        P(("rep", "member", "tp"), None),
        P(("rep", "member", "tp")),
        P(),
        P("member", None, "tp"),
        P("member", "tp", None),
        P(),
        P(),
    )
    out_specs = (P(("rep", "member", "tp"), None), P(("rep", "member", "tp"), None))
    return jax.shard_map(local, mesh=mesh, in_specs=in_specs, out_specs=out_specs, check_vma=False)
```

profile of v0, /device:TPU:0, one launch (start us, length us, event | category | flops | bytes accessed | tf_op | source)
XLA Modules:
  0.0 118.7 jit_solution(594228416031735746)
XLA Ops:
  7.2 0.7 and_select_fusion
  8.4 0.8 select_reduce_fusion.1
  9.6 0.8 gather_fusion
  10.6 0.8 pad_maximum_fusion
  11.8 3.0 %collective-permute-start.2 = (bf16[1024,256]{1,0:T(8,128)(2,1)S(1)}, bf16[1024,256]{1,0:T(8,128)(2,1)S(1)}, u32[]{:S(2)}, u32[]{:S(2)}) collective-permute-start(bf16[1024,256]{1,0:T(8,128)(2,1)S(1)} %dynamic-slice_bitcast_fusion), channel_id=1, source_target_pairs={{0,8},{4,12},{8,0},{12,4},{1,9},{5,13},{9,1},{13,5},{2,10},{6,14},... | collective-permute-start | bytes 1572872 | tf_op jit(solution)/shard_map/ppermute | solution.py:15
  14.8 11.9 %collective-permute-done.2 = bf16[1024,256]{1,0:T(8,128)(2,1)S(1)} collective-permute-done((bf16[1024,256]{1,0:T(8,128)(2,1)S(1)}, bf16[1024,256]{1,0:T(8,128)(2,1)S(1)}, u32[]{:S(2)}, u32[]{:S(2)}) %collective-permute-start.2) | collective-permute-done | bytes 524320 | tf_op jit(solution)/shard_map/ppermute | solution.py:15
  26.8 1.8 %collective-permute-start.6 = (bf16[256,1024]{1,0:T(8,128)(2,1)S(1)}, bf16[256,1024]{1,0:T(8,128)(2,1)}, u32[]{:S(2)}, u32[]{:S(2)}) collective-permute-start(bf16[256,1024]{1,0:T(8,128)(2,1)S(1)} %constant_dynamic-slice_fusion), channel_id=1, source_target_pairs={{0,8},{4,12},{8,0},{12,4},{1,9},{5,13},{9,1},{13,5},{2,10},{6,14},... | collective-permute-start | bytes 1572872 | tf_op jit(solution)/shard_map/ppermute | solution.py:15
  28.6 1.5 %collective-permute-start.3 = (bf16[1024,256]{1,0:T(8,128)(2,1)S(1)}, bf16[1024,256]{1,0:T(8,128)(2,1)}, u32[]{:S(2)}, u32[]{:S(2)}) collective-permute-start(bf16[1024,256]{1,0:T(8,128)(2,1)S(1)} %collective-permute-done.2), channel_id=1, source_target_pairs={{0,16},{16,0},{1,17},{17,1},{2,18},{18,2},{3,19},{19,3},{4,20},{20... | collective-permute-start | bytes 1572872 | tf_op jit(solution)/shard_map/ppermute | solution.py:21
  30.1 10.1 %collective-permute-done.6 = bf16[256,1024]{1,0:T(8,128)(2,1)} collective-permute-done((bf16[256,1024]{1,0:T(8,128)(2,1)S(1)}, bf16[256,1024]{1,0:T(8,128)(2,1)}, u32[]{:S(2)}, u32[]{:S(2)}) %collective-permute-start.6) | collective-permute-done | bytes 524320 | tf_op jit(solution)/shard_map/ppermute | solution.py:15
  40.2 1.4 %collective-permute-start.7 = (bf16[256,1024]{1,0:T(8,128)(2,1)}, bf16[256,1024]{1,0:T(8,128)(2,1)}, u32[]{:S(2)}, u32[]{:S(2)}) collective-permute-start(bf16[256,1024]{1,0:T(8,128)(2,1)} %collective-permute-done.6), channel_id=1, source_target_pairs={{0,16},{16,0},{1,17},{17,1},{2,18},{18,2},{3,19},{19,3},{4,20},{20... | collective-permute-start | bytes 1572872 | tf_op jit(solution)/shard_map/ppermute | solution.py:21
  41.6 3.1 %all-gather.2.cloned.1.call-done = bf16[512,1152]{1,0:T(8,128)(2,1)} async-done(((bf16[128,1152]{1,0:T(8,128)(2,1)}), bf16[512,1152]{1,0:T(8,128)(2,1)}) %all-gather.2.cloned.1.call-update) | async-done | bytes 1179664 | tf_op jit(solution)/shard_map/all_gather | solution.py:83
  44.7 1.1 fusion.84
  45.8 0.5 collective-permute-start.5
  46.3 7.9 %collective-permute-done.7 = bf16[256,1024]{1,0:T(8,128)(2,1)} collective-permute-done((bf16[256,1024]{1,0:T(8,128)(2,1)}, bf16[256,1024]{1,0:T(8,128)(2,1)}, u32[]{:S(2)}, u32[]{:S(2)}) %collective-permute-start.7) | collective-permute-done | bytes 524320 | tf_op jit(solution)/shard_map/ppermute | solution.py:21
  54.3 4.9 %fusion.20 = f32[512,1024]{1,0:T(8,128)S(1)} fusion(bf16[512,1024]{1,0:T(8,128)(2,1)} %collective-permute-done.1, bf16[512,1024]{1,0:T(8,128)(2,1)} %bitcast.38, bf16[1024,512]{1,0:T(8,128)(2,1)} %collective-permute-done, bf16[1024,512]{1,0:T(8,128)(2,1)} %bitcast.41, bf16[512,1152]{1,0:T(8,128)(2,1)} %all-gather.2.cloned.1.call-done, ...), kind=kOutput, calls=%fused_computation.23 | convolution fusion | flops 2161115136 | bytes 7341056 | tf_op jit(solution)/shard_map/dot_general | solution.py:97
  59.2 6.0 %fusion.32 = f32[512,1024]{1,0:T(8,128)} fusion(bf16[256,1024]{1,0:T(8,128)(2,1)} %collective-permute-done.9, bf16[256,1024]{1,0:T(8,128)(2,1)} %collective-permute-done.8, bf16[256,1024]{1,0:T(8,128)(2,1)} %collective-permute-done.7, bf16[256,1024]{1,0:T(8,128)(2,1)} %collective-permute-done.6, bf16[1024,256]{1,0:T(8,128)(2,1)} %collective-permute-done.5, ...), kind=kOutput, calls=%fused_computation.35 | convolution fusion | flops 2169503744 | bytes 7341056 | tf_op jit(solution)/shard_map/dot_general | solution.py:97
  65.3 2.3 %fusion.75 = (bf16[128,1024]{1,0:T(8,128)(2,1)S(1)}, bf16[128,1024]{1,0:T(8,128)(2,1)}, bf16[128,1024]{1,0:T(8,128)(2,1)S(1)}) fusion(f32[4,128,1024]{2,1,0:T(8,128)} %bitcast.34, s32[]{:T(128)S(6)} %select_n.91, f32[4,128,1024]{2,1,0:T(8,128)S(1)} %bitcast.32, s32[]{:T(128)S(6)} %select_n.95, s32[]{:T(128)S(6)} %select_n.93), kind=kLoop, calls=%fused_computation.77 | loop fusion | flops 786432 | bytes 3932172 | tf_op jit(solution)/shard_map/convert_element_type | solution.py:125
  67.5 3.6 %collective-permute-start.12 = (bf16[128,1024]{1,0:T(8,128)(2,1)}, bf16[128,1024]{1,0:T(8,128)(2,1)}, u32[]{:S(2)}, u32[]{:S(2)}) collective-permute-start(bf16[128,1024]{1,0:T(8,128)(2,1)} %get-tuple-element.29), channel_id=1, source_target_pairs={{0,3},{1,0},{2,1},{3,2},{4,7},{5,4},{6,5},{7,6},{8,11},{9,8},{10,9... | collective-permute-start | bytes 786440 | tf_op jit(solution)/shard_map/ppermute | solution.py:124
  71.1 1.0 collective-permute-start.10
  72.2 6.0 %collective-permute-done.12 = bf16[128,1024]{1,0:T(8,128)(2,1)} collective-permute-done((bf16[128,1024]{1,0:T(8,128)(2,1)}, bf16[128,1024]{1,0:T(8,128)(2,1)}, u32[]{:S(2)}, u32[]{:S(2)}) %collective-permute-start.12) | collective-permute-done | bytes 262176 | tf_op jit(solution)/shard_map/ppermute | solution.py:124
  78.2 16.3 %collective-permute-done.11 = bf16[128,1024]{1,0:T(8,128)(2,1)} collective-permute-done((bf16[128,1024]{1,0:T(8,128)(2,1)S(1)}, bf16[128,1024]{1,0:T(8,128)(2,1)}, u32[]{:S(2)}, u32[]{:S(2)}) %collective-permute-start.11) | collective-permute-done | bytes 262176 | tf_op jit(solution)/shard_map/ppermute | solution.py:124
  94.5 1.5 %fusion.72 = bf16[128,1024]{1,0:T(8,128)(2,1)S(1)} fusion(f32[128,1024]{1,0:T(8,128)S(1)} %get-tuple-element.36, bf16[128,1024]{1,0:T(8,128)(2,1)} %collective-permute-done.12, bf16[128,1024]{1,0:T(8,128)(2,1)} %collective-permute-done.11, bf16[128,1024]{1,0:T(8,128)(2,1)} %collective-permute-done.10, f32[4,128,1024]{2,1,0:T(8,128)} %bitcast.35, ...), kind=kLoop, calls=%fused_computation.64 | loop fusion | flops 1179648 | bytes 2621444 | tf_op jit(solution)/shard_map/convert_element_type | solution.py:129
  96.0 14.5 %all_to_all.5 = bf16[16,8,1152]{2,1,0:T(8,128)(2,1)S(1)} all-to-all(bf16[16,8,1152]{2,1,0:T(8,128)(2,1)S(1)} %maximum_bitcast_fusion), channel_id=1, replica_groups=mesh['rep'=2,'member'=4,'tp'=4] {'member','tp'}, dimensions={0} | all-to-all | bytes 589824 | tf_op jit(solution)/shard_map/all_to_all | solution.py:133
  111.0 0.9 fusion.41
  (47 shorter events, 2.1 us)
Async XLA Ops:
  7.2 2.0 %copy-start = (bf16[128,1024]{1,0:T(8,128)(2,1)S(1)}, bf16[128,1024]{1,0:T(8,128)(2,1)}, u32[]{:S(2)}) copy-start(bf16[128,1024]{1,0:T(8,128)(2,1)} %param.8) | copy-start | bytes 786436
  7.2 2.4 %copy-start.1 = (f32[2,1024]{1,0:T(2,128)S(1)}, f32[2,1024]{1,0:T(2,128)}, u32[]{:S(2)}) copy-start(f32[2,1024]{1,0:T(2,128)} %param.11) | copy-start | bytes 24580
  7.2 37.5 %all-gather.2.cloned.1.call-start = ((), (), s32[]{:S(2)}) async-start(), calls=%async_computation.1 | async-start | bytes 1474560 | tf_op jit(solution)/shard_map/all_gather | solution.py:83
  10.4 1.3 %copy-start.3 = (bf16[1,1024,512]{2,1,0:T(8,128)(2,1)S(1)}, bf16[1,1024,512]{2,1,0:T(8,128)(2,1)}, u32[]{:S(2)}) copy-start(bf16[1,1024,512]{2,1,0:T(8,128)(2,1)} %param.12) | copy-start | bytes 3145732
  10.4 4.4 %copy-start.2 = (bf16[1,512,1024]{2,1,0:T(8,128)(2,1)S(1)}, bf16[1,512,1024]{2,1,0:T(8,128)(2,1)}, u32[]{:S(2)}) copy-start(bf16[1,512,1024]{2,1,0:T(8,128)(2,1)} %param.13) | copy-start | bytes 3145732
  11.8 15.0 %collective-permute-start.2 = (bf16[1024,256]{1,0:T(8,128)(2,1)S(1)}, bf16[1024,256]{1,0:T(8,128)(2,1)S(1)}, u32[]{:S(2)}, u32[]{:S(2)}) collective-permute-start(bf16[1024,256]{1,0:T(8,128)(2,1)S(1)} %dynamic-slice_bitcast_fusion), channel_id=1, source_target_pairs={{0,8},{4,12},{8,0},{12,4},{1,9},{5,13},{9,1},{13,5},{2,10},{6,14},... | collective-permute-start | bytes 1572872 | tf_op jit(solution)/shard_map/ppermute | solution.py:15
  14.8 30.9 %collective-permute-start.1 = (bf16[512,1024]{1,0:T(8,128)(2,1)S(1)}, bf16[512,1024]{1,0:T(8,128)(2,1)}, u32[]{:S(2)}, u32[]{:S(2)}) collective-permute-start(bf16[512,1024]{1,0:T(8,128)(2,1)S(1)} %bitcast.39), channel_id=1, source_target_pairs={{0,4},{4,0},{8,12},{12,8},{1,5},{5,1},{9,13},{13,9},{2,6},{6,2},{1... | collective-permute-start | bytes 3145736 | tf_op jit(solution)/shard_map/ppermute | solution.py:10
  26.8 13.4 %collective-permute-start.6 = (bf16[256,1024]{1,0:T(8,128)(2,1)S(1)}, bf16[256,1024]{1,0:T(8,128)(2,1)}, u32[]{:S(2)}, u32[]{:S(2)}) collective-permute-start(bf16[256,1024]{1,0:T(8,128)(2,1)S(1)} %constant_dynamic-slice_fusion), channel_id=1, source_target_pairs={{0,8},{4,12},{8,0},{12,4},{1,9},{5,13},{9,1},{13,5},{2,10},{6,14},... | collective-permute-start | bytes 1572872 | tf_op jit(solution)/shard_map/ppermute | solution.py:15
  28.6 25.7 %collective-permute-start = (bf16[1024,512]{1,0:T(8,128)(2,1)S(1)}, bf16[1024,512]{1,0:T(8,128)(2,1)}, u32[]{:S(2)}, u32[]{:S(2)}) collective-permute-start(bf16[1024,512]{1,0:T(8,128)(2,1)S(1)} %bitcast.42), channel_id=1, source_target_pairs={{0,4},{4,0},{8,12},{12,8},{1,5},{5,1},{9,13},{13,9},{2,6},{6,2},{1... | collective-permute-start | bytes 3145736 | tf_op jit(solution)/shard_map/ppermute | solution.py:10
  28.6 17.2 %collective-permute-start.3 = (bf16[1024,256]{1,0:T(8,128)(2,1)S(1)}, bf16[1024,256]{1,0:T(8,128)(2,1)}, u32[]{:S(2)}, u32[]{:S(2)}) collective-permute-start(bf16[1024,256]{1,0:T(8,128)(2,1)S(1)} %collective-permute-done.2), channel_id=1, source_target_pairs={{0,16},{16,0},{1,17},{17,1},{2,18},{18,2},{3,19},{19,3},{4,20},{20... | collective-permute-start | bytes 1572872 | tf_op jit(solution)/shard_map/ppermute | solution.py:21
  40.2 14.1 %collective-permute-start.7 = (bf16[256,1024]{1,0:T(8,128)(2,1)}, bf16[256,1024]{1,0:T(8,128)(2,1)}, u32[]{:S(2)}, u32[]{:S(2)}) collective-permute-start(bf16[256,1024]{1,0:T(8,128)(2,1)} %collective-permute-done.6), channel_id=1, source_target_pairs={{0,16},{16,0},{1,17},{17,1},{2,18},{18,2},{3,19},{19,3},{4,20},{20... | collective-permute-start | bytes 1572872 | tf_op jit(solution)/shard_map/ppermute | solution.py:21
  41.6 17.6 %collective-permute-start.4 = (bf16[1024,256]{1,0:T(8,128)(2,1)S(1)}, bf16[1024,256]{1,0:T(8,128)(2,1)}, u32[]{:S(2)}, u32[]{:S(2)}) collective-permute-start(bf16[1024,256]{1,0:T(8,128)(2,1)S(1)} %collective-permute-done.2), channel_id=1, source_target_pairs={{0,4},{4,0},{8,12},{12,8},{1,5},{5,1},{9,13},{13,9},{2,6},{6,2},{1... | collective-permute-start | bytes 1572872 | tf_op jit(solution)/shard_map/ppermute | solution.py:10
  45.8 13.5 %collective-permute-start.8 = (bf16[256,1024]{1,0:T(8,128)(2,1)}, bf16[256,1024]{1,0:T(8,128)(2,1)}, u32[]{:S(2)}, u32[]{:S(2)}) collective-permute-start(bf16[256,1024]{1,0:T(8,128)(2,1)} %collective-permute-done.6), channel_id=1, source_target_pairs={{0,4},{4,0},{8,12},{12,8},{1,5},{5,1},{9,13},{13,9},{2,6},{6,2},{1... | collective-permute-start | bytes 1572872 | tf_op jit(solution)/shard_map/ppermute | solution.py:10
  45.8 13.4 %collective-permute-start.5 = (bf16[1024,256]{1,0:T(8,128)(2,1)}, bf16[1024,256]{1,0:T(8,128)(2,1)}, u32[]{:S(2)}, u32[]{:S(2)}) collective-permute-start(bf16[1024,256]{1,0:T(8,128)(2,1)} %collective-permute-done.3), channel_id=1, source_target_pairs={{0,4},{4,0},{8,12},{12,8},{1,5},{5,1},{9,13},{13,9},{2,6},{6,2},{1... | collective-permute-start | bytes 1572872 | tf_op jit(solution)/shard_map/ppermute | solution.py:10
  54.3 5.0 %collective-permute-start.9 = (bf16[256,1024]{1,0:T(8,128)(2,1)}, bf16[256,1024]{1,0:T(8,128)(2,1)}, u32[]{:S(2)}, u32[]{:S(2)}) collective-permute-start(bf16[256,1024]{1,0:T(8,128)(2,1)} %collective-permute-done.7), channel_id=1, source_target_pairs={{0,4},{4,0},{8,12},{12,8},{1,5},{5,1},{9,13},{13,9},{2,6},{6,2},{1... | collective-permute-start | bytes 1572872 | tf_op jit(solution)/shard_map/ppermute | solution.py:10
  67.5 10.6 %collective-permute-start.12 = (bf16[128,1024]{1,0:T(8,128)(2,1)}, bf16[128,1024]{1,0:T(8,128)(2,1)}, u32[]{:S(2)}, u32[]{:S(2)}) collective-permute-start(bf16[128,1024]{1,0:T(8,128)(2,1)} %get-tuple-element.29), channel_id=1, source_target_pairs={{0,3},{1,0},{2,1},{3,2},{4,7},{5,4},{6,5},{7,6},{8,11},{9,8},{10,9... | collective-permute-start | bytes 786440 | tf_op jit(solution)/shard_map/ppermute | solution.py:124
  71.1 23.3 %collective-permute-start.11 = (bf16[128,1024]{1,0:T(8,128)(2,1)S(1)}, bf16[128,1024]{1,0:T(8,128)(2,1)}, u32[]{:S(2)}, u32[]{:S(2)}) collective-permute-start(bf16[128,1024]{1,0:T(8,128)(2,1)S(1)} %get-tuple-element.30), channel_id=1, source_target_pairs={{0,2},{1,3},{2,0},{3,1},{4,6},{5,7},{6,4},{7,5},{8,10},{9,11},{10,... | collective-permute-start | bytes 786440 | tf_op jit(solution)/shard_map/ppermute | solution.py:124
  71.1 23.3 %collective-permute-start.10 = (bf16[128,1024]{1,0:T(8,128)(2,1)S(1)}, bf16[128,1024]{1,0:T(8,128)(2,1)}, u32[]{:S(2)}, u32[]{:S(2)}) collective-permute-start(bf16[128,1024]{1,0:T(8,128)(2,1)S(1)} %get-tuple-element.28), channel_id=1, source_target_pairs={{0,1},{1,2},{2,3},{3,0},{4,5},{5,6},{6,7},{7,4},{8,9},{9,10},{10,1... | collective-permute-start | bytes 786440 | tf_op jit(solution)/shard_map/ppermute | solution.py:124
  72.2 38.8 %copy-start.4 = (bf16[1024,128]{1,0:T(8,128)(2,1)S(1)}, bf16[1024,128]{1,0:T(8,128)(2,1)}, u32[]{:S(2)}) copy-start(bf16[1024,128]{1,0:T(8,128)(2,1)} %param.15) | copy-start | bytes 786436
  72.2 38.8 %copy-start.5 = (f32[1024]{0:T(1024)S(1)}, f32[1024]{0:T(1024)}, u32[]{:S(2)}) copy-start(f32[1024]{0:T(1024)} %param.14) | copy-start | bytes 12292
  110.9 1.0 copy-start.6
Sparse Core Ops, SparseCore 0:
  11.5 33.1 all-gather.1
where the time goes:
time: 119 us
  waiting for transfers between devices  55.4 us (47%)
  blocking collectives  14.5 us (12%)
  between operations  14.3 us (12%)
  starting transfers between devices  12.9 us (11%)
  matrix products  12.5 us (11%)
  other arithmetic  7.9 us (7%)
  local copies, waits for them, and re-layouts  1.27 us (1%)
    ppermute x3, waiting for transfers between devices, local(): lax.ppermute(slice_for((tp_here + shift) % n_tp).astype(PARTIAL_DTYPE), '...  22.3 us
    ppermute x2, waiting for transfers between devices, from_chip_behind(): lax.ppermute(value, axis, [(i, (i + 2 * chips_back) % size) for i in rang...  22 us
    all_to_all x1, blocking collectives, local(): lax.all_to_all(jnp.concatenate([packed, spot_lanes], axis=1).reshape(n_de...  14.5 us
    dot_general x2, matrix products, apply_block(): return jnp.dot(hidden, down_here, preferred_element_type=jnp.float32)  10.9 us
    ppermute x2, waiting for transfers between devices, swap_parts(): lax.ppermute(value, 'rep', [(i, (i + step) % n_rep) for i in range(n_rep)])  7.94 us
    ppermute x2, starting transfers between devices, from_chip_behind(): lax.ppermute(value, axis, [(i, (i + 2 * chips_back) % size) for i in rang...  4.84 us
    ppermute x3, starting transfers between devices, local(): lax.ppermute(slice_for((tp_here + shift) % n_tp).astype(PARTIAL_DTYPE), '...  4.61 us
    all_gather x1, waiting for transfers between devices, local(): lax.all_gather(jnp.concatenate([normed, member_lanes], axis=1), 'tp', axi...  3.1 us
  transfers between devices with their start and end apart: 14, of which 6 were waited for; matrix products, arithmetic and copies ran while one was open for 5% of the time, Pallas kernels for 0%

commit v1 on v0

--- a/solution.py
+++ b/solution.py
@@ -4,6 +4,24 @@
 from jax.sharding import PartitionSpec as P
 
 PARTIAL_DTYPE = jnp.bfloat16
+
+
+def collect(array, axis, dim):
+    ways, here, step = (lax.axis_size(axis), lax.axis_index(axis), array.shape[dim])
+    shape = [n * ways if d == dim else n for d, n in enumerate(array.shape)]
+    full = lax.dynamic_update_slice_in_dim(
+        jnp.zeros(shape, array.dtype), array, here * step, axis=dim
+    )
+    going_up = going_down = array
+    for far in range(1, ways // 2 + 1):
+        going_up = lax.ppermute(going_up, axis, [(d, (d + 1) % ways) for d in range(ways)])
+        full = lax.dynamic_update_slice_in_dim(full, going_up, (here - far) % ways * step, axis=dim)
+        if 2 * far < ways:
+            going_down = lax.ppermute(going_down, axis, [(d, (d - 1) % ways) for d in range(ways)])
+            full = lax.dynamic_update_slice_in_dim(
+                full, going_down, (here + far) % ways * step, axis=dim
+            )
+    return full
 
 
 def from_partner(value, axis, distance):
@@ -80,9 +98,7 @@
     member_lanes = jnp.where(
         jnp.arange(128, dtype=jnp.int32)[None, :] == 0, member[:, None], 0
     ).astype(jnp.bfloat16)
-    gathered = lax.all_gather(
-        jnp.concatenate([normed, member_lanes], axis=1), "tp", axis=0, tiled=True
-    )
+    gathered = collect(jnp.concatenate([normed, member_lanes], axis=1), "tp", 0)
     gathered_rows = gathered[:, :feature_width]
     gathered_member = gathered[:, feature_width].astype(jnp.int32)
 

time: 119 us -> 116 us (0.975)
  between operations: 14.3 us -> 1.06 us
  local copies, waits for them, and re-layouts: 1.27 us -> 7.47 us
  starting transfers between devices: 12.9 us -> 18 us
  other arithmetic: 7.9 us -> 4.77 us
  blocking collectives: 14.5 us -> 16.2 us
    ppermute x2, waiting for transfers between devices: 22 us -> 7.06 us  [from_chip_behind(): lax.ppermute(value, axis, [(i, (i + 2 * chips_back) % size) for i in rang...]
    ppermute x0 -> x3, waiting for transfers between devices: none -> 9.83 us  [the longest x1 6.26 us: collect(): lax.ppermute(going_down, axis, [(d, (d - 1) % ways) for d in range(ways)])]
    ppermute x2, waiting for transfers between devices: 7.94 us -> 17.2 us  [swap_parts(): lax.ppermute(value, 'rep', [(i, (i + step) % n_rep) for i in range(n_rep)])]
    ppermute x0 -> x3, starting transfers between devices: none -> 5.29 us  [the longest x1 3.6 us: collect(): lax.ppermute(going_down, axis, [(d, (d - 1) % ways) for d in range(ways)])]
    all_gather x1 -> x0, waiting for transfers between devices: 3.1 us -> none  [local(): lax.all_gather(jnp.concatenate([normed, member_lanes], axis=1), 'tp', axi...]
    dot_general x0 -> x1, matrix products: none -> 3.1 us  [apply_block(): jnp.dot(gathered_rows, up_here, preferred_element_type=jnp.float32)]
    dot_general x2, matrix products: 10.9 us -> 8.09 us  [apply_block(): return jnp.dot(hidden, down_here, preferred_element_type=jnp.float32)]
    ppermute x0 -> x3, local copies, waits for them, and re-layouts: none -> 2.54 us  [the longest x2 1.38 us: collect(): lax.ppermute(going_up, axis, [(d, (d + 1) % ways) for d in range(ways)])]
  transfers between devices with their start and end apart: 14 -> 16, of which waited for: 6 -> 7; matrix products, arithmetic and copies ran while one was open for 5% -> 11% of each run, Pallas kernels for 0% -> 0%
where the time goes in v1:
time: 116 us; the launch traced here: 115 us
  waiting for transfers between devices  55 us (47%)
  starting transfers between devices  18 us (16%)
  blocking collectives  16.2 us (14%)
  matrix products  12.7 us (11%)
  local copies, waits for them, and re-layouts  7.47 us (6%)
  other arithmetic  4.77 us (4%)
    ppermute x3, waiting for transfers between devices, local(): lax.ppermute(slice_for((tp_here + shift) % n_tp).astype(PARTIAL_DTYPE), '...  20.9 us
    ppermute x2, waiting for transfers between devices, swap_parts(): lax.ppermute(value, 'rep', [(i, (i + step) % n_rep) for i in range(n_rep)])  17.2 us
    all_to_all x1, blocking collectives, local(): lax.all_to_all(jnp.concatenate([packed, spot_lanes], axis=1).reshape(n_de...  16.2 us
    dot_general x2, matrix products, apply_block(): return jnp.dot(hidden, down_here, preferred_element_type=jnp.float32)  8.09 us
    ppermute x2, waiting for transfers between devices, from_chip_behind(): lax.ppermute(value, axis, [(i, (i + 2 * chips_back) % size) for i in rang...  7.06 us
    ppermute x1, waiting for transfers between devices, collect(): lax.ppermute(going_down, axis, [(d, (d - 1) % ways) for d in range(ways)])  6.26 us
    ppermute x3, starting transfers between devices, local(): lax.ppermute(slice_for((tp_here + shift) % n_tp).astype(PARTIAL_DTYPE), '...  4.95 us
    ppermute x2, starting transfers between devices, from_chip_behind(): lax.ppermute(value, axis, [(i, (i + 2 * chips_back) % size) for i in rang...  4.84 us
  transfers between devices with their start and end apart: 16, of which 7 were waited for; matrix products, arithmetic and copies ran while one was open for 11% of the time, Pallas kernels for 0%

profile of v1, /device:TPU:0, one launch (start us, length us, event | category | flops | bytes accessed | tf_op | source)
XLA Modules:
  0.0 115.2 jit_solution(17275557341946204100)
XLA Ops:
  0.7 1.1 dynamic-slice_bitcast_fusion
  1.8 3.0 %collective-permute-start.5 = (bf16[1024,256]{1,0:T(8,128)(2,1)S(1)}, bf16[1024,256]{1,0:T(8,128)(2,1)}, u32[]{:S(2)}, u32[]{:S(2)}) collective-permute-start(bf16[1024,256]{1,0:T(8,128)(2,1)S(1)} %dynamic-slice_bitcast_fusion), channel_id=1, source_target_pairs={{0,8},{4,12},{8,0},{12,4},{1,9},{5,13},{9,1},{13,5},{2,10},{6,14},... | collective-permute-start | bytes 1572872 | tf_op jit(solution)/shard_map/ppermute | solution.py:33
  8.2 1.6 %collective-permute-start = (bf16[128,1152]{1,0:T(8,128)(2,1)S(1)}, bf16[128,1152]{1,0:T(8,128)(2,1)S(1)}, u32[]{:S(2)}, u32[]{:S(2)}) collective-permute-start(bf16[128,1152]{1,0:T(8,128)(2,1)S(1)} %pad_maximum_fusion), channel_id=1, source_target_pairs={{0,1},{1,2},{2,3},{3,0},{4,5},{5,6},{6,7},{7,4},{8,9},{9,10},{10,1... | collective-permute-start | bytes 884744 | tf_op jit(solution)/shard_map/ppermute | solution.py:17
  9.8 7.1 %collective-permute-done.5 = bf16[1024,256]{1,0:T(8,128)(2,1)} collective-permute-done((bf16[1024,256]{1,0:T(8,128)(2,1)S(1)}, bf16[1024,256]{1,0:T(8,128)(2,1)}, u32[]{:S(2)}, u32[]{:S(2)}) %collective-permute-start.5) | collective-permute-done | bytes 524320 | tf_op jit(solution)/shard_map/ppermute | solution.py:33
  16.8 1.1 constant_dynamic-slice_fusion
  17.9 1.8 %collective-permute-start.9 = (bf16[256,1024]{1,0:T(8,128)(2,1)S(1)}, bf16[256,1024]{1,0:T(8,128)(2,1)}, u32[]{:S(2)}, u32[]{:S(2)}) collective-permute-start(bf16[256,1024]{1,0:T(8,128)(2,1)S(1)} %constant_dynamic-slice_fusion), channel_id=1, source_target_pairs={{0,8},{4,12},{8,0},{12,4},{1,9},{5,13},{9,1},{13,5},{2,10},{6,14},... | collective-permute-start | bytes 1572872 | tf_op jit(solution)/shard_map/ppermute | solution.py:33
  19.7 3.6 %collective-permute-start.1 = (bf16[128,1152]{1,0:T(8,128)(2,1)S(1)}, bf16[128,1152]{1,0:T(8,128)(2,1)}, u32[]{:S(2)}, u32[]{:S(2)}) collective-permute-start(bf16[128,1152]{1,0:T(8,128)(2,1)S(1)} %pad_maximum_fusion), channel_id=1, source_target_pairs={{0,3},{1,0},{2,1},{3,2},{4,7},{5,4},{6,5},{7,6},{8,11},{9,8},{10,9... | collective-permute-start | bytes 884744 | tf_op jit(solution)/shard_map/ppermute | solution.py:20
  24.4 6.3 %collective-permute-done.1 = bf16[128,1152]{1,0:T(8,128)(2,1)} collective-permute-done((bf16[128,1152]{1,0:T(8,128)(2,1)S(1)}, bf16[128,1152]{1,0:T(8,128)(2,1)}, u32[]{:S(2)}, u32[]{:S(2)}) %collective-permute-start.1) | collective-permute-done | bytes 294944 | tf_op jit(solution)/shard_map/ppermute | solution.py:20
  30.7 1.2 %copy.17 = bf16[128,1152]{0,1:T(8,128)(2,1)S(1)} copy(bf16[128,1152]{1,0:T(8,128)(2,1)} %collective-permute-done.1) | data formatting | bytes 589824 | tf_op jit(solution)/shard_map/ppermute | solution.py:20
  31.9 1.6 %collective-permute-start.6 = (bf16[1024,256]{1,0:T(8,128)(2,1)}, bf16[1024,256]{1,0:T(8,128)(2,1)}, u32[]{:S(2)}, u32[]{:S(2)}) collective-permute-start(bf16[1024,256]{1,0:T(8,128)(2,1)} %collective-permute-done.5), channel_id=1, source_target_pairs={{0,16},{16,0},{1,17},{17,1},{2,18},{18,2},{3,19},{19,3},{4,20},{20... | collective-permute-start | bytes 1572872 | tf_op jit(solution)/shard_map/ppermute | solution.py:39
  34.0 3.6 %collective-permute-done.2 = bf16[128,1152]{1,0:T(8,128)(2,1)} collective-permute-done((bf16[128,1152]{1,0:T(8,128)(2,1)S(1)}, bf16[128,1152]{1,0:T(8,128)(2,1)}, u32[]{:S(2)}, u32[]{:S(2)}) %collective-permute-start.2) | collective-permute-done | bytes 294944 | tf_op jit(solution)/shard_map/ppermute | solution.py:17
  37.6 1.2 %copy.18 = bf16[128,1152]{0,1:T(8,128)(2,1)S(1)} copy(bf16[128,1152]{1,0:T(8,128)(2,1)} %collective-permute-done.2) | data formatting | bytes 589824 | tf_op jit(solution)/shard_map/ppermute | solution.py:17
  39.5 7.6 %collective-permute-done.6 = bf16[1024,256]{1,0:T(8,128)(2,1)} collective-permute-done((bf16[1024,256]{1,0:T(8,128)(2,1)}, bf16[1024,256]{1,0:T(8,128)(2,1)}, u32[]{:S(2)}, u32[]{:S(2)}) %collective-permute-start.6) | collective-permute-done | bytes 524320 | tf_op jit(solution)/shard_map/ppermute | solution.py:39
  47.1 9.5 %collective-permute-done.10 = bf16[256,1024]{1,0:T(8,128)(2,1)} collective-permute-done((bf16[256,1024]{1,0:T(8,128)(2,1)}, bf16[256,1024]{1,0:T(8,128)(2,1)}, u32[]{:S(2)}, u32[]{:S(2)}) %collective-permute-start.10) | collective-permute-done | bytes 524320 | tf_op jit(solution)/shard_map/ppermute | solution.py:39
  56.7 5.1 %fusion.20 = f32[512,1024]{1,0:T(8,128)S(1)} fusion(bf16[512,1024]{1,0:T(8,128)(2,1)} %collective-permute-done.4, bf16[512,1024]{1,0:T(8,128)(2,1)} %bitcast.4, bf16[1024,512]{1,0:T(8,128)(2,1)} %collective-permute-done.3, bf16[1024,512]{1,0:T(8,128)(2,1)} %bitcast.3, bf16[512,1152]{0,1:T(8,128)(2,1)} %copy-done.3, bf16[512]{0:T(512)(128)(2,1)S(1)} %get-tuple-element.25), kind=kOutput, calls=%fused_computation.23 | convolution fusion | flops 2161115136 | bytes 7341056 | tf_op jit(solution)/shard_map/dot_general | solution.py:113
  61.8 3.1 %fusion.24 = f32[512,1024]{1,0:T(8,128)S(1)} fusion(bf16[1024,256]{1,0:T(8,128)(2,1)} %collective-permute-done.8, bf16[1024,256]{1,0:T(8,128)(2,1)} %collective-permute-done.7, bf16[1024,256]{1,0:T(8,128)(2,1)} %collective-permute-done.6, bf16[1024,256]{1,0:T(8,128)(2,1)} %collective-permute-done.5, bf16[512,1152]{0,1:T(8,128)(2,1)} %copy-done.3), kind=kOutput, calls=%fused_computation.27 | convolution fusion | flops 1082130432 | bytes 5242880 | tf_op jit(solution)/shard_map/dot_general | solution.py:108
  64.9 3.0 %fusion.32 = f32[512,1024]{1,0:T(8,128)S(1)} fusion(bf16[256,1024]{1,0:T(8,128)(2,1)} %collective-permute-done.12, bf16[256,1024]{1,0:T(8,128)(2,1)} %collective-permute-done.11, bf16[256,1024]{1,0:T(8,128)(2,1)} %collective-permute-done.10, bf16[256,1024]{1,0:T(8,128)(2,1)} %collective-permute-done.9, f32[512,1024]{1,0:T(8,128)S(1)} %fusion.24, ...), kind=kOutput, calls=%fused_computation.35 | convolution fusion | flops 1087373312 | bytes 6292480 | tf_op jit(solution)/shard_map/dot_general | solution.py:113
  67.9 1.3 %copy-done.2 = f32[512,1024]{1,0:T(8,128)} copy-done((f32[512,1024]{1,0:T(8,128)}, f32[512,1024]{1,0:T(8,128)S(1)}, u32[]{:S(2)}) %copy-start.2) | copy-done | bytes 2097176
  69.2 1.0 fusion.67
  70.2 4.4 %collective-permute-start.15 = (bf16[128,1024]{1,0:T(8,128)(2,1)}, bf16[128,1024]{1,0:T(8,128)(2,1)}, u32[]{:S(2)}, u32[]{:S(2)}) collective-permute-start(bf16[128,1024]{1,0:T(8,128)(2,1)} %get-tuple-element.29), channel_id=1, source_target_pairs={{0,3},{1,0},{2,1},{3,2},{4,7},{5,4},{6,5},{7,6},{8,11},{9,8},{10,9... | collective-permute-start | bytes 786440 | tf_op jit(solution)/shard_map/ppermute | solution.py:140
  75.2 6.5 %collective-permute-done.15 = bf16[128,1024]{1,0:T(8,128)(2,1)} collective-permute-done((bf16[128,1024]{1,0:T(8,128)(2,1)}, bf16[128,1024]{1,0:T(8,128)(2,1)}, u32[]{:S(2)}, u32[]{:S(2)}) %collective-permute-start.15) | collective-permute-done | bytes 262176 | tf_op jit(solution)/shard_map/ppermute | solution.py:140
  81.6 14.4 %collective-permute-done.14 = bf16[128,1024]{1,0:T(8,128)(2,1)} collective-permute-done((bf16[128,1024]{1,0:T(8,128)(2,1)S(1)}, bf16[128,1024]{1,0:T(8,128)(2,1)}, u32[]{:S(2)}, u32[]{:S(2)}) %collective-permute-start.14) | collective-permute-done | bytes 262176 | tf_op jit(solution)/shard_map/ppermute | solution.py:140
  96.0 1.5 %fusion.64 = bf16[128,1024]{1,0:T(8,128)(2,1)S(1)} fusion(f32[128,1024]{1,0:T(8,128)S(1)} %get-tuple-element.36, bf16[128,1024]{1,0:T(8,128)(2,1)} %collective-permute-done.15, bf16[128,1024]{1,0:T(8,128)(2,1)} %collective-permute-done.14, bf16[128,1024]{1,0:T(8,128)(2,1)} %collective-permute-done.13, f32[4,128,1024]{2,1,0:T(8,128)} %bitcast.35, ...), kind=kLoop, calls=%fused_computation.64 | loop fusion | flops 1179648 | bytes 2621444 | tf_op jit(solution)/shard_map/convert_element_type | solution.py:145
  97.6 16.2 %all_to_all.5 = bf16[16,8,1152]{2,1,0:T(8,128)(2,1)S(1)} all-to-all(bf16[16,8,1152]{2,1,0:T(8,128)(2,1)S(1)} %maximum_bitcast_fusion), channel_id=1, replica_groups=mesh['rep'=2,'member'=4,'tp'=4] {'member','tp'}, dimensions={0} | all-to-all | bytes 589824 | tf_op jit(solution)/shard_map/all_to_all | solution.py:149
  (60 shorter events, 7.5 us)
Async XLA Ops:
  0.6 6.1 %copy-start = (bf16[128,1024]{1,0:T(8,128)(2,1)S(1)}, bf16[128,1024]{1,0:T(8,128)(2,1)}, u32[]{:S(2)}) copy-start(bf16[128,1024]{1,0:T(8,128)(2,1)} %param.8) | copy-start | bytes 786436
  0.6 6.5 %copy-start.1 = (f32[2,1024]{1,0:T(2,128)S(1)}, f32[2,1024]{1,0:T(2,128)}, u32[]{:S(2)}) copy-start(f32[2,1024]{1,0:T(2,128)} %param.11) | copy-start | bytes 24580
  1.8 15.1 %collective-permute-start.5 = (bf16[1024,256]{1,0:T(8,128)(2,1)S(1)}, bf16[1024,256]{1,0:T(8,128)(2,1)}, u32[]{:S(2)}, u32[]{:S(2)}) collective-permute-start(bf16[1024,256]{1,0:T(8,128)(2,1)S(1)} %dynamic-slice_bitcast_fusion), channel_id=1, source_target_pairs={{0,8},{4,12},{8,0},{12,4},{1,9},{5,13},{9,1},{13,5},{2,10},{6,14},... | collective-permute-start | bytes 1572872 | tf_op jit(solution)/shard_map/ppermute | solution.py:33
  8.2 15.9 %collective-permute-start = (bf16[128,1152]{1,0:T(8,128)(2,1)S(1)}, bf16[128,1152]{1,0:T(8,128)(2,1)S(1)}, u32[]{:S(2)}, u32[]{:S(2)}) collective-permute-start(bf16[128,1152]{1,0:T(8,128)(2,1)S(1)} %pad_maximum_fusion), channel_id=1, source_target_pairs={{0,1},{1,2},{2,3},{3,0},{4,5},{5,6},{6,7},{7,4},{8,9},{9,10},{10,1... | collective-permute-start | bytes 884744 | tf_op jit(solution)/shard_map/ppermute | solution.py:17
  17.9 15.5 %collective-permute-start.9 = (bf16[256,1024]{1,0:T(8,128)(2,1)S(1)}, bf16[256,1024]{1,0:T(8,128)(2,1)}, u32[]{:S(2)}, u32[]{:S(2)}) collective-permute-start(bf16[256,1024]{1,0:T(8,128)(2,1)S(1)} %constant_dynamic-slice_fusion), channel_id=1, source_target_pairs={{0,8},{4,12},{8,0},{12,4},{1,9},{5,13},{9,1},{13,5},{2,10},{6,14},... | collective-permute-start | bytes 1572872 | tf_op jit(solution)/shard_map/ppermute | solution.py:33
  19.7 19.2 %collective-permute-start.4 = (bf16[512,1024]{1,0:T(8,128)(2,1)}, bf16[512,1024]{1,0:T(8,128)(2,1)}, u32[]{:S(2)}, u32[]{:S(2)}) collective-permute-start(bf16[512,1024]{1,0:T(8,128)(2,1)} %bitcast.4), channel_id=1, source_target_pairs={{0,4},{4,0},{8,12},{12,8},{1,5},{5,1},{9,13},{13,9},{2,6},{6,2},{1... | collective-permute-start | bytes 3145736 | tf_op jit(solution)/shard_map/ppermute | solution.py:28
  19.7 11.0 %collective-permute-start.1 = (bf16[128,1152]{1,0:T(8,128)(2,1)S(1)}, bf16[128,1152]{1,0:T(8,128)(2,1)}, u32[]{:S(2)}, u32[]{:S(2)}) collective-permute-start(bf16[128,1152]{1,0:T(8,128)(2,1)S(1)} %pad_maximum_fusion), channel_id=1, source_target_pairs={{0,3},{1,0},{2,1},{3,2},{4,7},{5,4},{6,5},{7,6},{8,11},{9,8},{10,9... | collective-permute-start | bytes 884744 | tf_op jit(solution)/shard_map/ppermute | solution.py:20
  23.3 33.3 %collective-permute-start.3 = (bf16[1024,512]{1,0:T(8,128)(2,1)}, bf16[1024,512]{1,0:T(8,128)(2,1)}, u32[]{:S(2)}, u32[]{:S(2)}) collective-permute-start(bf16[1024,512]{1,0:T(8,128)(2,1)} %bitcast.3), channel_id=1, source_target_pairs={{0,4},{4,0},{8,12},{12,8},{1,5},{5,1},{9,13},{13,9},{2,6},{6,2},{1... | collective-permute-start | bytes 3145736 | tf_op jit(solution)/shard_map/ppermute | solution.py:28
  24.3 13.3 %collective-permute-start.2 = (bf16[128,1152]{1,0:T(8,128)(2,1)S(1)}, bf16[128,1152]{1,0:T(8,128)(2,1)}, u32[]{:S(2)}, u32[]{:S(2)}) collective-permute-start(bf16[128,1152]{1,0:T(8,128)(2,1)S(1)} %collective-permute-done), channel_id=1, source_target_pairs={{0,1},{1,2},{2,3},{3,0},{4,5},{5,6},{6,7},{7,4},{8,9},{9,10},{10,1... | collective-permute-start | bytes 884744 | tf_op jit(solution)/shard_map/ppermute | solution.py:17
  31.9 15.2 %collective-permute-start.6 = (bf16[1024,256]{1,0:T(8,128)(2,1)}, bf16[1024,256]{1,0:T(8,128)(2,1)}, u32[]{:S(2)}, u32[]{:S(2)}) collective-permute-start(bf16[1024,256]{1,0:T(8,128)(2,1)} %collective-permute-done.5), channel_id=1, source_target_pairs={{0,16},{16,0},{1,17},{17,1},{2,18},{18,2},{3,19},{19,3},{4,20},{20... | collective-permute-start | bytes 1572872 | tf_op jit(solution)/shard_map/ppermute | solution.py:39
  33.4 23.2 %collective-permute-start.10 = (bf16[256,1024]{1,0:T(8,128)(2,1)}, bf16[256,1024]{1,0:T(8,128)(2,1)}, u32[]{:S(2)}, u32[]{:S(2)}) collective-permute-start(bf16[256,1024]{1,0:T(8,128)(2,1)} %collective-permute-done.9), channel_id=1, source_target_pairs={{0,16},{16,0},{1,17},{17,1},{2,18},{18,2},{3,19},{19,3},{4,20},{20... | collective-permute-start | bytes 1572872 | tf_op jit(solution)/shard_map/ppermute | solution.py:39
  37.6 24.1 %collective-permute-start.7 = (bf16[1024,256]{1,0:T(8,128)(2,1)}, bf16[1024,256]{1,0:T(8,128)(2,1)}, u32[]{:S(2)}, u32[]{:S(2)}) collective-permute-start(bf16[1024,256]{1,0:T(8,128)(2,1)} %collective-permute-done.5), channel_id=1, source_target_pairs={{0,4},{4,0},{8,12},{12,8},{1,5},{5,1},{9,13},{13,9},{2,6},{6,2},{1... | collective-permute-start | bytes 1572872 | tf_op jit(solution)/shard_map/ppermute | solution.py:28
  38.9 17.8 %copy-start.3 = (bf16[512,1152]{0,1:T(8,128)(2,1)}, bf16[512,1152]{0,1:T(8,128)(2,1)S(1)}, u32[]{:S(2)}) copy-start(bf16[512,1152]{0,1:T(8,128)(2,1)S(1)} %constant_dynamic-update-slice_fusion) | copy-start | bytes 3538948
  38.9 22.8 %collective-permute-start.11 = (bf16[256,1024]{1,0:T(8,128)(2,1)}, bf16[256,1024]{1,0:T(8,128)(2,1)}, u32[]{:S(2)}, u32[]{:S(2)}) collective-permute-start(bf16[256,1024]{1,0:T(8,128)(2,1)} %collective-permute-done.9), channel_id=1, source_target_pairs={{0,4},{4,0},{8,12},{12,8},{1,5},{5,1},{9,13},{13,9},{2,6},{6,2},{1... | collective-permute-start | bytes 1572872 | tf_op jit(solution)/shard_map/ppermute | solution.py:28
  47.1 14.6 %collective-permute-start.8 = (bf16[1024,256]{1,0:T(8,128)(2,1)}, bf16[1024,256]{1,0:T(8,128)(2,1)}, u32[]{:S(2)}, u32[]{:S(2)}) collective-permute-start(bf16[1024,256]{1,0:T(8,128)(2,1)} %collective-permute-done.6), channel_id=1, source_target_pairs={{0,4},{4,0},{8,12},{12,8},{1,5},{5,1},{9,13},{13,9},{2,6},{6,2},{1... | collective-permute-start | bytes 1572872 | tf_op jit(solution)/shard_map/ppermute | solution.py:28
  56.7 5.1 %collective-permute-start.12 = (bf16[256,1024]{1,0:T(8,128)(2,1)}, bf16[256,1024]{1,0:T(8,128)(2,1)}, u32[]{:S(2)}, u32[]{:S(2)}) collective-permute-start(bf16[256,1024]{1,0:T(8,128)(2,1)} %collective-permute-done.10), channel_id=1, source_target_pairs={{0,4},{4,0},{8,12},{12,8},{1,5},{5,1},{9,13},{13,9},{2,6},{6,2},{1... | collective-permute-start | bytes 1572872 | tf_op jit(solution)/shard_map/ppermute | solution.py:28
  67.9 1.3 %copy-start.2 = (f32[512,1024]{1,0:T(8,128)}, f32[512,1024]{1,0:T(8,128)S(1)}, u32[]{:S(2)}) copy-start(f32[512,1024]{1,0:T(8,128)S(1)} %fusion.32) | copy-start | bytes 6291460
  70.2 11.4 %collective-permute-start.15 = (bf16[128,1024]{1,0:T(8,128)(2,1)}, bf16[128,1024]{1,0:T(8,128)(2,1)}, u32[]{:S(2)}, u32[]{:S(2)}) collective-permute-start(bf16[128,1024]{1,0:T(8,128)(2,1)} %get-tuple-element.29), channel_id=1, source_target_pairs={{0,3},{1,0},{2,1},{3,2},{4,7},{5,4},{6,5},{7,6},{8,11},{9,8},{10,9... | collective-permute-start | bytes 786440 | tf_op jit(solution)/shard_map/ppermute | solution.py:140
  74.6 21.4 %collective-permute-start.14 = (bf16[128,1024]{1,0:T(8,128)(2,1)S(1)}, bf16[128,1024]{1,0:T(8,128)(2,1)}, u32[]{:S(2)}, u32[]{:S(2)}) collective-permute-start(bf16[128,1024]{1,0:T(8,128)(2,1)S(1)} %get-tuple-element.30), channel_id=1, source_target_pairs={{0,2},{1,3},{2,0},{3,1},{4,6},{5,7},{6,4},{7,5},{8,10},{9,11},{10,... | collective-permute-start | bytes 786440 | tf_op jit(solution)/shard_map/ppermute | solution.py:140
  74.6 21.4 %collective-permute-start.13 = (bf16[128,1024]{1,0:T(8,128)(2,1)S(1)}, bf16[128,1024]{1,0:T(8,128)(2,1)}, u32[]{:S(2)}, u32[]{:S(2)}) collective-permute-start(bf16[128,1024]{1,0:T(8,128)(2,1)S(1)} %get-tuple-element.28), channel_id=1, source_target_pairs={{0,1},{1,2},{2,3},{3,0},{4,5},{5,6},{6,7},{7,4},{8,9},{9,10},{10,1... | collective-permute-start | bytes 786440 | tf_op jit(solution)/shard_map/ppermute | solution.py:140
  75.1 39.1 %copy-start.4 = (bf16[1024,128]{1,0:T(8,128)(2,1)S(1)}, bf16[1024,128]{1,0:T(8,128)(2,1)}, u32[]{:S(2)}) copy-start(bf16[1024,128]{1,0:T(8,128)(2,1)} %param.15) | copy-start | bytes 786436
  75.2 39.1 %copy-start.5 = (f32[1024]{0:T(1024)S(1)}, f32[1024]{0:T(1024)}, u32[]{:S(2)}) copy-start(f32[1024]{0:T(1024)} %param.14) | copy-start | bytes 12292
  114.2 1.0 copy-start.6
